TPU v7x, 32 devices: a whole 2x2x4 slice. The times are simulated.
32 devices in a mesh: req: 16 (over z, x, core), ep: 2 (over y).
Axes of the slice: x: 2, y: 2, z: 4, core: 2. Of those that a mesh axis runs over, the one named last changes fastest.
Arguments:
- hidden: bfloat16 [16, 512, 1536], P('req', None, 'ep'), may hold values from -6 to 6
- key_cache: bfloat16 [16, 8, 2560, 64], P('req', 'ep'), may hold values from -160 to 160
- value_cache: bfloat16 [16, 8, 2560, 64], P('req', 'ep'), may hold values from -6 to 6
- request_order: int32 [16], replicated, may hold values from 0 to 15, each once
- cached_lengths: int32 [16], replicated, may hold values from 1 to 2048, 16384 in all
- expert_ids: int32 [16, 512, 8], P('req'), may hold values from 0 to 39, all different within a row; in each aligned block of 512 rows (0 to 511, 512 to 1023, ..., all dimensions but the last counted through in order) at most 192 rows name the same one
- gate_values: float32 [16, 512, 8], P('req'), may hold values from 0.1 to 1
- attn_gain: float32 [1536], replicated, may hold values from 0.25 to 1.75
- ffn_gain: float32 [1536], replicated, may hold values from 0.25 to 1.75
- w_query: bfloat16 [1536, 1536], P(None, 'ep'), may hold values from -0.15625 to 0.15625
- w_key: bfloat16 [1536, 512], P(None, 'ep'), may hold values from -0.15625 to 0.15625
- w_value: bfloat16 [1536, 512], P(None, 'ep'), may hold values from -0.15625 to 0.15625
- w_out: bfloat16 [1536, 1536], P('ep'), may hold values from -0.15625 to 0.15625
- expert_gate: bfloat16 [4, 1536, 512], P('ep', 'req'), may hold values from -0.15625 to 0.15625
- expert_up: bfloat16 [4, 1536, 512], P('ep', 'req'), may hold values from -0.15625 to 0.15625
- expert_down: bfloat16 [4, 512, 1536], P('ep', 'req'), may hold values from -0.25 to 0.25
Outputs:
- hidden_out: bfloat16 [16, 512, 1536], P('req', None, 'ep')
- key_cache_out: bfloat16 [16, 8, 2560, 64], P('req', 'ep')
- value_cache_out: bfloat16 [16, 8, 2560, 64], P('req', 'ep')
Inputs may be any that keep to these rules, and one draw needn't show every extreme that they name: Slot s holds request request_order[s]; every request is held by one slot. `cached_lengths`: the longest cached length is exactly 2048. `expert_ids`: each token names 8 different experts; among the 512 tokens of one slot no expert is named by more than 192 tokens, a bound that some block reaches.
All inputs are finite; a program needn't handle non-finite values.
Results may differ from a plain program's by a relative error of at most 0.012.
The roundings to bfloat16 on the way count: a program that leaves them out, or rounds other values in their place, can miss the bound.
Values may be sent and summed in bfloat16 or wider, within the bound.
No kernel may reach another device: no remote copies, remote signals or barrier semaphores. Data moves between devices by JAX's collectives and lax.ppermute only.
A program may use at most 128 MiB of HBM per device.

v0:
```python
import jax
import jax.numpy as jnp
from jax import lax
from jax.sharding import PartitionSpec as P

epsilon = 1e-06


def normalize(values, gain):
    return values * lax.rsqrt(jnp.mean(values * values, -1, keepdims=True) + epsilon) * gain


def rotate(values, positions):
    half = values.shape[-1] // 2
    freq = 10000.0 ** (-jnp.arange(half, dtype=jnp.float32) * (2.0 / values.shape[-1]))
    angle = positions.astype(jnp.float32)[:, None] * freq[None, :]
    cosine = jnp.cos(angle)
    sine = jnp.sin(angle)
    first = values[..., :half]
    second = values[..., half:]
    return jnp.concatenate([first * cosine - second * sine, second * cosine + first * sine], -1)


def rounded(values):
    return lax.optimization_barrier(values.astype(jnp.bfloat16)).astype(jnp.float32)


def route_tables(chosen, gate_rows, wanted, capacity):
    hits = chosen[:, :, None] == wanted[None, None, :]
    member = jnp.sum(hits.astype(jnp.int32), 1, dtype=jnp.int32)
    weight = jnp.sum(jnp.where(hits, gate_rows[:, :, None], 0.0), 1)
    place = jnp.cumsum(member, 0, dtype=jnp.int32) - 1
    slots = jnp.arange(capacity, dtype=jnp.int32)
    table = (member.T[:, None, :] == 1) & (place.T[:, None, :] == slots[None, :, None])
    gate_slot = jnp.sum(jnp.where(table, weight.T[:, None, :], 0.0), 2)
    return (table.astype(jnp.bfloat16), gate_slot)


def attend(query, keys, values, length, new_rows):
    query_rows = query.shape[1]
    blocks = keys.shape[1] // new_rows
    limit = length + jnp.arange(query_rows, dtype=jnp.int32) % new_rows
    scale = query.shape[2] ** (-0.5)

    def visit(carry, block):
        running, total, summed = carry
        start = block * new_rows
        key_block = lax.dynamic_slice_in_dim(keys, start, new_rows, 1)
        value_block = lax.dynamic_slice_in_dim(values, start, new_rows, 1)
        scores = (
            jnp.einsum("kqd,kjd->kqj", query, key_block, preferred_element_type=jnp.float32) * scale
        )
        column = start + jnp.arange(new_rows, dtype=jnp.int32)
        visible = column[None, :] <= limit[:, None]
        scores = jnp.where(visible[None], scores, -1e30)
        highest = jnp.maximum(running, jnp.max(scores, -1))
        correction = jnp.exp(running - highest)
        probs = jnp.where(visible[None], jnp.exp(scores - highest[..., None]), 0.0)
        total = total * correction + jnp.sum(probs, -1)
        summed = summed * correction[..., None] + jnp.einsum(
            "kqj,kjd->kqd",
            probs.astype(jnp.bfloat16),
            value_block,
            preferred_element_type=jnp.float32,
        )
        return ((highest, total, summed), None)

    start_state = (
        jnp.full(query.shape[:2], -1e30, jnp.float32),
        jnp.zeros(query.shape[:2], jnp.float32),
        jnp.zeros(query.shape, jnp.float32),
    )
    final, unused = lax.scan(visit, start_state, jnp.arange(blocks, dtype=jnp.int32))
    return final[2] / final[1][..., None]


def on_device(
    hidden,
    key_cache,
    value_cache,
    request_order,
    cached_lengths,
    expert_ids,
    gate_values,
    attn_gain,
    ffn_gain,
    w_query,
    w_key,
    w_value,
    w_out,
    expert_gate,
    expert_up,
    expert_down,
):
    own_rows = hidden[0]
    new_rows = own_rows.shape[0]
    own_width = own_rows.shape[1]
    head_dim = key_cache.shape[3]
    kv_local = key_cache.shape[1]
    heads_local = w_query.shape[1] // head_dim
    group = heads_local // kv_local
    per_device = expert_gate.shape[0]
    devices = lax.axis_size("ep")
    capacity = 3 * new_rows // 8
    everyone = jnp.arange(request_order.shape[0], dtype=jnp.int32)
    request = jnp.sum(jnp.where(everyone == lax.axis_index("req"), request_order, 0))
    length = jnp.sum(jnp.where(everyone == request, cached_lengths, 0))
    rows_whole = lax.all_gather(own_rows, "ep", axis=1, tiled=True)
    width = rows_whole.shape[1]
    normed = normalize(rows_whole.astype(jnp.float32), attn_gain).astype(jnp.bfloat16)
    query = jnp.dot(normed, w_query, preferred_element_type=jnp.float32)
    key_new = jnp.dot(normed, w_key, preferred_element_type=jnp.float32)
    value_new = jnp.dot(normed, w_value, preferred_element_type=jnp.float32)
    positions = length + jnp.arange(new_rows, dtype=jnp.int32)
    query = rotate(
        query.reshape(new_rows, heads_local, head_dim).transpose(1, 0, 2), positions
    ).astype(jnp.bfloat16)
    query = query.reshape(kv_local, group * new_rows, head_dim)
    key_new = rotate(
        key_new.reshape(new_rows, kv_local, head_dim).transpose(1, 0, 2), positions
    ).astype(jnp.bfloat16)
    value_new = (
        value_new.reshape(new_rows, kv_local, head_dim).transpose(1, 0, 2).astype(jnp.bfloat16)
    )
    zero = jnp.zeros((), jnp.int32)
    keys = lax.dynamic_update_slice(key_cache[0], key_new, (zero, length, zero))
    values = lax.dynamic_update_slice(value_cache[0], value_new, (zero, length, zero))
    attended = attend(query, keys, values, length, new_rows)
    attended = (
        attended.reshape(heads_local, new_rows, head_dim)
        .transpose(1, 0, 2)
        .reshape(new_rows, heads_local * head_dim)
        .astype(jnp.bfloat16)
    )
    partial_value = rounded(jnp.dot(attended, w_out, preferred_element_type=jnp.float32))
    head_sum = lax.psum_scatter(
        partial_value.astype(jnp.bfloat16), "ep", scatter_dimension=1, tiled=True
    ).astype(jnp.float32)
    mixed = (own_rows.astype(jnp.float32) + head_sum).astype(jnp.bfloat16)
    mixed_f = mixed.astype(jnp.float32)
    chosen = expert_ids[0]
    gate_rows = gate_values[0]
    first = lax.axis_index("ep") * per_device
    squares = jnp.sum(mixed_f * mixed_f, -1)
    totals = lax.psum(squares, "ep")
    local_gain = lax.dynamic_slice_in_dim(ffn_gain, lax.axis_index("ep") * own_width, own_width)
    normed_cols = (mixed_f * lax.rsqrt(totals / width + epsilon)[:, None] * local_gain).astype(
        jnp.bfloat16
    )
    table_all, gate_all = route_tables(
        chosen, gate_rows, jnp.arange(per_device * devices, dtype=jnp.int32), capacity
    )
    buffers = jnp.einsum(
        "ect,td->ecd", table_all, normed_cols, preferred_element_type=jnp.float32
    ).astype(jnp.bfloat16)
    inputs = lax.all_to_all(buffers, "ep", split_axis=0, concat_axis=2, tiled=True)
    gate_own = lax.dynamic_slice_in_dim(gate_all, first, per_device, 0)
    columns = inputs
    gate_next = jnp.einsum(
        "ecd,edf->ecf",
        columns,
        lax.all_gather(expert_gate, "req", axis=1, tiled=True),
        preferred_element_type=jnp.float32,
    )
    up_next = jnp.einsum(
        "ecd,edf->ecf",
        columns,
        lax.all_gather(expert_up, "req", axis=1, tiled=True),
        preferred_element_type=jnp.float32,
    )
    hidden_act = (jax.nn.silu(gate_next) * up_next).astype(jnp.bfloat16)
    columns = hidden_act
    output = jnp.einsum(
        "ecf,efd->ecd",
        columns,
        lax.all_gather(expert_down, "req", axis=1, tiled=True),
        preferred_element_type=jnp.float32,
    )
    contrib = (output * gate_own[..., None]).astype(jnp.bfloat16)
    returned = lax.all_to_all(contrib, "ep", split_axis=2, concat_axis=0, tiled=True)
    per_expert = jnp.einsum("ect,ecd->etd", table_all, returned, preferred_element_type=jnp.float32)
    grouped = rounded(jnp.sum(per_expert.reshape(devices, per_device, new_rows, own_width), 1))
    expert_sum = jnp.sum(grouped, 0)
    result = (mixed_f + expert_sum).astype(jnp.bfloat16)
    return (result[None], keys[None], values[None])


def solution(mesh):
    in_specs = (
        P("req", None, "ep"),
        P("req", "ep", None, None),
        P("req", "ep", None, None),
        P(),
        P(),
        P("req", None, None),
        P("req", None, None),
        P(),
        P(),
        P(None, "ep"),
        P(None, "ep"),
        P(None, "ep"),
        P("ep", None),
        P("ep", "req", None),
        P("ep", "req", None),
        P("ep", "req", None),
    )
    out_specs = (P("req", None, "ep"), P("req", "ep", None, None), P("req", "ep", None, None))
    return jax.shard_map(
        on_device, mesh=mesh, in_specs=in_specs, out_specs=out_specs, check_vma=False
    )
```

profile of v0, /device:TPU:0, one launch (start us, length us, event | category | flops | bytes accessed | tf_op | source)
XLA Modules:
  0.0 390.4 jit_solution(1194642636352865639)
XLA Ops:
  8.1 2.6 copy.81
  16.7 25.2 %all-gather.12.cloned.1.call-done = bf16[1,512,1536]{2,1,0:T(8,128)(2,1)} async-done(((bf16[1,512,768]{2,1,0:T(8,128)(2,1)}), bf16[1,512,1536]{2,1,0:T(8,128)(2,1)}) %all-gather.12.cloned.1.call-update) | async-done | bytes 1572880 | tf_op jit(solution)/shard_map/all_gather | solution.py:108
  54.8 4.0 %dynamic_update_slice.6 = bf16[4,2560,64]{1,2,0:T(8,128)(2,1)} dynamic-update-slice(bf16[4,2560,64]{1,2,0:T(8,128)(2,1)} %bitcast.102, bf16[4,512,64]{1,2,0:T(8,128)(2,1)S(1)} %pad_maximum_fusion.1, s32[]{:T(128)} %constant.31.clone.1, s32[]{:T(128)S(6)} %select_n.46, s32[]{:T(128)} %constant.31.clone.1) | dynamic-update-slice | bytes 524292 | tf_op jit(solution)/shard_map/dynamic_update_slice | solution.py:126
  61.1 3.8 dynamic_update_slice.7
  64.9 123.9 %while.15 = (s32[]{:T(128)}, f32[4,1536]{1,0:T(4,128)S(1)}, f32[4,1536]{1,0:T(4,128)S(1)}, f32[4,1536,64]{1,2,0:T(8,128)}, s32[5]{0:T(128)S(1)}, /*index=5*/bf16...) while((s32[]{:T(128)}, f32[4,1536]{1,0:T(4,128)S(1)}, ...), condition=%wide.region_6.7_spmd.clone, body=%wide.region_3.6_spmd.clone.sunk | while | flops 848208896 | bytes 96092400 | solution.py:73
  67.5 8.1 %fusion.93 = (f32[4,1536]{1,0:T(4,128)S(1)}, f32[4,512,1536]{2,1,0:T(8,128)}) fusion(pred[1536,512]{0,1:T(8,128)(4,1)S(1)} %broadcast_compare_fusion.3, bf16[4,1536,64]{1,2,0:T(8,128)(2,1)} %get-tuple-element.236, bf16[4,2560,64]{1,2,0:T(8,128)(2,1)} %get-tuple-element.235, s32[]{:T(128)S(6)} %select_n.102), kind=kOutput, calls=%fused_computation.3.clone.1 | convolution fusion | flops 412084224 | bytes 14442500 | tf_op jit(solution)/shard_map/while/body/eval_jaxpr/kqd,kjd->kqj/dot_general | solution.py:51
  75.6 6.9 %fusion.94 = f32[4,1536]{1,0:T(4,128)S(1)} fusion(f32[4,512,1536]{2,1,0:T(8,128)} %get-tuple-element.201, f32[4,1536]{1,0:T(4,128)S(1)} %select_maximum_fusion.2, pred[1536,512]{0,1:T(8,128)(4,1)S(1)} %broadcast_compare_fusion.3), kind=kLoop, calls=%fused_computation.5.clone.1 | loop fusion | flops 15722496 | bytes 13418496 | tf_op jit(solution)/shard_map/while/body/eval_jaxpr/reduce_sum | solution.py:59
  83.8 5.7 %fusion.96 = f32[4,1536,64]{1,2,0:T(8,128)} fusion(f32[4,512,1536]{2,1,0:T(8,128)S(1)} %copy-done.1, f32[4,1536]{1,0:T(4,128)S(1)} %select_maximum_fusion.2, pred[1536,512]{0,1:T(8,128)(4,1)S(1)} %broadcast_compare_fusion.3, f32[4,1536,64]{1,2,0:T(8,128)} %get-tuple-element.220, f32[4,1536]{1,0:T(4,128)S(1)} %get-tuple-element.203, pred[]{:T(512)S(6)} %compare.4, ...), kind=kOutput, calls=%fused_computation.8.clone.1 | convolution fusion | flops 419561472 | bytes 16826372 | tf_op jit(solution)/shard_map/while/body/eval_jaxpr/kqj,kjd->kqd/dot_general | solution.py:60
  92.1 8.1 %fusion.93 = (f32[4,1536]{1,0:T(4,128)S(1)}, f32[4,512,1536]{2,1,0:T(8,128)}) fusion(pred[1536,512]{0,1:T(8,128)(4,1)S(1)} %broadcast_compare_fusion.3, bf16[4,1536,64]{1,2,0:T(8,128)(2,1)} %get-tuple-element.236, bf16[4,2560,64]{1,2,0:T(8,128)(2,1)} %get-tuple-element.235, s32[]{:T(128)S(6)} %select_n.102), kind=kOutput, calls=%fused_computation.3.clone.1 | convolution fusion | flops 412084224 | bytes 14442500 | tf_op jit(solution)/shard_map/while/body/eval_jaxpr/kqd,kjd->kqj/dot_general | solution.py:51
  100.1 6.9 %fusion.94 = f32[4,1536]{1,0:T(4,128)S(1)} fusion(f32[4,512,1536]{2,1,0:T(8,128)} %get-tuple-element.201, f32[4,1536]{1,0:T(4,128)S(1)} %select_maximum_fusion.2, pred[1536,512]{0,1:T(8,128)(4,1)S(1)} %broadcast_compare_fusion.3), kind=kLoop, calls=%fused_computation.5.clone.1 | loop fusion | flops 15722496 | bytes 13418496 | tf_op jit(solution)/shard_map/while/body/eval_jaxpr/reduce_sum | solution.py:59
  108.4 6.0 %fusion.96 = f32[4,1536,64]{1,2,0:T(8,128)} fusion(f32[4,512,1536]{2,1,0:T(8,128)S(1)} %copy-done.1, f32[4,1536]{1,0:T(4,128)S(1)} %select_maximum_fusion.2, pred[1536,512]{0,1:T(8,128)(4,1)S(1)} %broadcast_compare_fusion.3, f32[4,1536,64]{1,2,0:T(8,128)} %get-tuple-element.220, f32[4,1536]{1,0:T(4,128)S(1)} %get-tuple-element.203, pred[]{:T(512)S(6)} %compare.4, ...), kind=kOutput, calls=%fused_computation.8.clone.1 | convolution fusion | flops 419561472 | bytes 16826372 | tf_op jit(solution)/shard_map/while/body/eval_jaxpr/kqj,kjd->kqd/dot_general | solution.py:60
  116.9 8.1 %fusion.93 = (f32[4,1536]{1,0:T(4,128)S(1)}, f32[4,512,1536]{2,1,0:T(8,128)}) fusion(pred[1536,512]{0,1:T(8,128)(4,1)S(1)} %broadcast_compare_fusion.3, bf16[4,1536,64]{1,2,0:T(8,128)(2,1)} %get-tuple-element.236, bf16[4,2560,64]{1,2,0:T(8,128)(2,1)} %get-tuple-element.235, s32[]{:T(128)S(6)} %select_n.102), kind=kOutput, calls=%fused_computation.3.clone.1 | convolution fusion | flops 412084224 | bytes 14442500 | tf_op jit(solution)/shard_map/while/body/eval_jaxpr/kqd,kjd->kqj/dot_general | solution.py:51
  125.0 6.9 %fusion.94 = f32[4,1536]{1,0:T(4,128)S(1)} fusion(f32[4,512,1536]{2,1,0:T(8,128)} %get-tuple-element.201, f32[4,1536]{1,0:T(4,128)S(1)} %select_maximum_fusion.2, pred[1536,512]{0,1:T(8,128)(4,1)S(1)} %broadcast_compare_fusion.3), kind=kLoop, calls=%fused_computation.5.clone.1 | loop fusion | flops 15722496 | bytes 13418496 | tf_op jit(solution)/shard_map/while/body/eval_jaxpr/reduce_sum | solution.py:59
  133.2 6.0 %fusion.96 = f32[4,1536,64]{1,2,0:T(8,128)} fusion(f32[4,512,1536]{2,1,0:T(8,128)S(1)} %copy-done.1, f32[4,1536]{1,0:T(4,128)S(1)} %select_maximum_fusion.2, pred[1536,512]{0,1:T(8,128)(4,1)S(1)} %broadcast_compare_fusion.3, f32[4,1536,64]{1,2,0:T(8,128)} %get-tuple-element.220, f32[4,1536]{1,0:T(4,128)S(1)} %get-tuple-element.203, pred[]{:T(512)S(6)} %compare.4, ...), kind=kOutput, calls=%fused_computation.8.clone.1 | convolution fusion | flops 419561472 | bytes 16826372 | tf_op jit(solution)/shard_map/while/body/eval_jaxpr/kqj,kjd->kqd/dot_general | solution.py:60
  141.7 8.1 %fusion.93 = (f32[4,1536]{1,0:T(4,128)S(1)}, f32[4,512,1536]{2,1,0:T(8,128)}) fusion(pred[1536,512]{0,1:T(8,128)(4,1)S(1)} %broadcast_compare_fusion.3, bf16[4,1536,64]{1,2,0:T(8,128)(2,1)} %get-tuple-element.236, bf16[4,2560,64]{1,2,0:T(8,128)(2,1)} %get-tuple-element.235, s32[]{:T(128)S(6)} %select_n.102), kind=kOutput, calls=%fused_computation.3.clone.1 | convolution fusion | flops 412084224 | bytes 14442500 | tf_op jit(solution)/shard_map/while/body/eval_jaxpr/kqd,kjd->kqj/dot_general | solution.py:51
  149.8 6.9 %fusion.94 = f32[4,1536]{1,0:T(4,128)S(1)} fusion(f32[4,512,1536]{2,1,0:T(8,128)} %get-tuple-element.201, f32[4,1536]{1,0:T(4,128)S(1)} %select_maximum_fusion.2, pred[1536,512]{0,1:T(8,128)(4,1)S(1)} %broadcast_compare_fusion.3), kind=kLoop, calls=%fused_computation.5.clone.1 | loop fusion | flops 15722496 | bytes 13418496 | tf_op jit(solution)/shard_map/while/body/eval_jaxpr/reduce_sum | solution.py:59
  158.1 6.0 %fusion.96 = f32[4,1536,64]{1,2,0:T(8,128)} fusion(f32[4,512,1536]{2,1,0:T(8,128)S(1)} %copy-done.1, f32[4,1536]{1,0:T(4,128)S(1)} %select_maximum_fusion.2, pred[1536,512]{0,1:T(8,128)(4,1)S(1)} %broadcast_compare_fusion.3, f32[4,1536,64]{1,2,0:T(8,128)} %get-tuple-element.220, f32[4,1536]{1,0:T(4,128)S(1)} %get-tuple-element.203, pred[]{:T(512)S(6)} %compare.4, ...), kind=kOutput, calls=%fused_computation.8.clone.1 | convolution fusion | flops 419561472 | bytes 16826372 | tf_op jit(solution)/shard_map/while/body/eval_jaxpr/kqj,kjd->kqd/dot_general | solution.py:60
  166.6 8.1 %fusion.93 = (f32[4,1536]{1,0:T(4,128)S(1)}, f32[4,512,1536]{2,1,0:T(8,128)}) fusion(pred[1536,512]{0,1:T(8,128)(4,1)S(1)} %broadcast_compare_fusion.3, bf16[4,1536,64]{1,2,0:T(8,128)(2,1)} %get-tuple-element.236, bf16[4,2560,64]{1,2,0:T(8,128)(2,1)} %get-tuple-element.235, s32[]{:T(128)S(6)} %select_n.102), kind=kOutput, calls=%fused_computation.3.clone.1 | convolution fusion | flops 412084224 | bytes 14442500 | tf_op jit(solution)/shard_map/while/body/eval_jaxpr/kqd,kjd->kqj/dot_general | solution.py:51
  174.7 6.9 %fusion.94 = f32[4,1536]{1,0:T(4,128)S(1)} fusion(f32[4,512,1536]{2,1,0:T(8,128)} %get-tuple-element.201, f32[4,1536]{1,0:T(4,128)S(1)} %select_maximum_fusion.2, pred[1536,512]{0,1:T(8,128)(4,1)S(1)} %broadcast_compare_fusion.3), kind=kLoop, calls=%fused_computation.5.clone.1 | loop fusion | flops 15722496 | bytes 13418496 | tf_op jit(solution)/shard_map/while/body/eval_jaxpr/reduce_sum | solution.py:59
  182.9 6.0 %fusion.96 = f32[4,1536,64]{1,2,0:T(8,128)} fusion(f32[4,512,1536]{2,1,0:T(8,128)S(1)} %copy-done.1, f32[4,1536]{1,0:T(4,128)S(1)} %select_maximum_fusion.2, pred[1536,512]{0,1:T(8,128)(4,1)S(1)} %broadcast_compare_fusion.3, f32[4,1536,64]{1,2,0:T(8,128)} %get-tuple-element.220, f32[4,1536]{1,0:T(4,128)S(1)} %get-tuple-element.203, pred[]{:T(512)S(6)} %compare.4, ...), kind=kOutput, calls=%fused_computation.8.clone.1 | convolution fusion | flops 419561472 | bytes 16826372 | tf_op jit(solution)/shard_map/while/body/eval_jaxpr/kqj,kjd->kqd/dot_general | solution.py:60
  200.4 22.6 %reduce-scatter.2.cloned.1.call-done = bf16[512,768]{1,0:T(8,128)(2,1)} async-done(((bf16[512,1536]{1,0:T(8,128)(2,1)}), bf16[512,768]{1,0:T(8,128)(2,1)}) %reduce-scatter.2.cloned.1.call-update) | async-done | bytes 786448 | tf_op jit(solution)/shard_map/reduce_scatter | solution.py:136
  224.5 5.2 %psum.7 = f32[512]{0:T(512)S(1)} all-reduce(f32[512]{0:T(512)S(1)} %fusion.28), channel_id=1, replica_groups=mesh['req'=16,'ep'=2] {'ep'}, use_global_device_ids=true, to_apply=%region_12.13 | all-reduce | flops 512 | bytes 4096 | tf_op jit(solution)/shard_map/psum | solution.py:145
  229.7 3.2 fusion.40
  232.9 4.6 %all-to-all-start = ((bf16[4,192,768]{2,1,0:T(8,128)(2,1)}), bf16[4,192,768]{2,1,0:T(8,128)(2,1)}, u32[]{:S(2)}, u32[]{:S(2)}) async-start(bf16[4,192,768]{2,1,0:T(8,128)(2,1)} %fusion.40), calls=%async_computation.1 | async-start | bytes 2359296 | tf_op jit(solution)/shard_map/all_to_all | solution.py:156
  238.0 14.2 %all-to-all-done = bf16[4,192,768]{2,1,0:T(8,128)(2,1)} async-done(((bf16[4,192,768]{2,1,0:T(8,128)(2,1)}), bf16[4,192,768]{2,1,0:T(8,128)(2,1)}, u32[]{:S(2)}, u32[]{:S(2)}) %all-to-all-start) | async-done | bytes 1179680 | tf_op jit(solution)/shard_map/all_to_all | solution.py:156
  254.6 3.9 %fusion.68 = f32[2,192,512]{2,1,0:T(8,128)} fusion(bf16[2,192,1536]{2,1,0:T(8,128)(2,1)} %bitcast.104, bf16[2,1536,512]{2,1,0:T(8,128)(2,1)} %all-gather.6.cloned.1.call-done), kind=kOutput, calls=%fused_computation.100 | convolution fusion | flops 603979776 | bytes 5111808 | tf_op jit(solution)/shard_map/ecd,edf->ecf/dot_general | solution.py:159
  258.5 32.5 %all-gather.10.cloned.1.call-done = bf16[2,512,1536]{2,1,0:T(8,128)(2,1)} async-done(((bf16[2,32,1536]{2,1,0:T(8,128)(2,1)}), bf16[2,512,1536]{2,1,0:T(8,128)(2,1)}) %all-gather.10.cloned.1.call-update) | async-done | bytes 3145744 | tf_op jit(solution)/shard_map/all_gather | solution.py:176
  291.0 46.1 %all-gather.8.cloned.1.call-done = bf16[2,1536,512]{2,1,0:T(8,128)(2,1)} async-done(((bf16[2,96,512]{2,1,0:T(8,128)(2,1)}), bf16[2,1536,512]{2,1,0:T(8,128)(2,1)}) %all-gather.8.cloned.1.call-update) | async-done | bytes 3145744 | tf_op jit(solution)/shard_map/all_gather | solution.py:168
  337.2 5.9 %fusion.27 = bf16[2,192,1536]{2,1,0:T(8,128)(2,1)} fusion(bf16[2,512,1536]{2,1,0:T(8,128)(2,1)} %all-gather.10.cloned.1.call-done, f32[2,192]{1,0:T(2,128)S(1)} %constant_dynamic-slice_fusion, bf16[2,192,1536]{2,1,0:T(8,128)(2,1)} %bitcast.105, bf16[2,1536,512]{2,1,0:T(8,128)(2,1)} %all-gather.8.cloned.1.call-done, f32[2,192,512]{2,1,0:T(8,128)} %fusion.68), kind=kOutput, calls=%fused_computation.39 | convolution fusion | flops 1210318848 | bytes 9438720 | tf_op jit(solution)/shard_map/ecf,efd->ecd/dot_general | solution.py:173
  343.1 4.8 %copy.57 = bf16[2,192,1536]{1,0,2:T(2,128)(2,1)} copy(bf16[2,192,1536]{2,1,0:T(8,128)(2,1)} %fusion.27) | data formatting | bytes 2359296 | tf_op jit(solution)/shard_map/convert_element_type | solution.py:179
  347.9 25.2 %all_to_all.36 = bf16[2,192,1536]{1,0,2:T(2,128)(2,1)} all-to-all(bf16[2,192,1536]{1,0,2:T(2,128)(2,1)} %copy.57), channel_id=1, replica_groups=mesh['req'=16,'ep'=2] {'ep'}, dimensions={2} | all-to-all | bytes 2359296 | tf_op jit(solution)/shard_map/all_to_all | solution.py:180
  373.1 4.9 %copy.58 = bf16[2,192,2,768]{3,1,0,2:T(8,128)(2,1)} copy(bf16[2,192,2,768]{1,0,3,2:T(2,128)(2,1)} %bitcast.101) | data formatting | bytes 2359296 | tf_op jit(solution)/shard_map/all_to_all | solution.py:180
  (127 shorter events, 56.0 us)
Async XLA Ops:
  8.0 186.2 %copy-start = (bf16[768,1536]{1,0:T(8,128)(2,1)S(1)}, bf16[768,1536]{1,0:T(8,128)(2,1)}, u32[]{:S(2)}) copy-start(bf16[768,1536]{1,0:T(8,128)(2,1)} %param.30) | copy-start | bytes 7077892
  8.0 33.8 %all-gather.12.cloned.1.call-start = ((), (), s32[]{:S(2)}) async-start(), calls=%async_computation.7 | async-start | bytes 2359296 | tf_op jit(solution)/shard_map/all_gather | solution.py:108
  8.1 2.6 copy-start.5
  10.7 1.2 copy-start.11
  10.7 1.8 copy-start.12
  11.8 32.0 %copy-start.10 = (f32[1536]{0:T(1024)S(1)}, f32[1536]{0:T(1024)}, u32[]{:S(2)}) copy-start(f32[1536]{0:T(1024)} %param.25) | copy-start | bytes 18436
  11.8 211.3 %reduce-scatter.2.cloned.1.call-start = ((), (), s32[]{:S(2)}) async-start(), calls=%async_computation.3 | async-start | bytes 2359296 | tf_op jit(solution)/shard_map/reduce_scatter | solution.py:136
  41.8 1.9 copy-start.4
  43.8 2.2 copy-start.9
  75.6 8.3 %copy-start.1 = (f32[4,512,1536]{2,1,0:T(8,128)S(1)}, f32[4,512,1536]{2,1,0:T(8,128)}, u32[]{:S(2)}) copy-start(f32[4,512,1536]{2,1,0:T(8,128)} %get-tuple-element.201) | copy-start | bytes 37748740 | tf_op jit(solution)/shard_map/while
  100.1 8.3 %copy-start.1 = (f32[4,512,1536]{2,1,0:T(8,128)S(1)}, f32[4,512,1536]{2,1,0:T(8,128)}, u32[]{:S(2)}) copy-start(f32[4,512,1536]{2,1,0:T(8,128)} %get-tuple-element.201) | copy-start | bytes 37748740 | tf_op jit(solution)/shard_map/while
  125.0 8.3 %copy-start.1 = (f32[4,512,1536]{2,1,0:T(8,128)S(1)}, f32[4,512,1536]{2,1,0:T(8,128)}, u32[]{:S(2)}) copy-start(f32[4,512,1536]{2,1,0:T(8,128)} %get-tuple-element.201) | copy-start | bytes 37748740 | tf_op jit(solution)/shard_map/while
  149.8 8.3 %copy-start.1 = (f32[4,512,1536]{2,1,0:T(8,128)S(1)}, f32[4,512,1536]{2,1,0:T(8,128)}, u32[]{:S(2)}) copy-start(f32[4,512,1536]{2,1,0:T(8,128)} %get-tuple-element.201) | copy-start | bytes 37748740 | tf_op jit(solution)/shard_map/while
  174.7 8.3 %copy-start.1 = (f32[4,512,1536]{2,1,0:T(8,128)S(1)}, f32[4,512,1536]{2,1,0:T(8,128)}, u32[]{:S(2)}) copy-start(f32[4,512,1536]{2,1,0:T(8,128)} %get-tuple-element.201) | copy-start | bytes 37748740 | tf_op jit(solution)/shard_map/while
  196.8 1.8 copy-start.6
  196.8 3.5 copy-start.8
  196.8 26.3 %copy-start.2 = (bf16[1,512,768]{2,1,0:T(8,128)(2,1)S(1)}, bf16[1,512,768]{2,1,0:T(8,128)(2,1)}, u32[]{:S(2)}) copy-start(bf16[1,512,768]{2,1,0:T(8,128)(2,1)} %param.18) | copy-start | bytes 2359300
  196.8 57.7 %all-gather.6.cloned.1.call-start = ((), (), s32[]{:S(2)}) async-start(), calls=%async_computation.4 | async-start | bytes 3342336 | tf_op jit(solution)/shard_map/all_gather | solution.py:162
  197.4 93.6 %all-gather.10.cloned.1.call-start = ((), (), s32[]{:S(2)}) async-start(), calls=%async_computation.6 | async-start | bytes 3342336 | tf_op jit(solution)/shard_map/all_gather | solution.py:176
  198.0 139.2 %all-gather.8.cloned.1.call-start = ((), (), s32[]{:S(2)}) async-start(), calls=%async_computation.5 | async-start | bytes 3342336 | tf_op jit(solution)/shard_map/all_gather | solution.py:168
  232.9 4.6 %copy-start.7 = (f32[1,512,8]{1,2,0:T(8,128)S(1)}, f32[1,512,8]{1,2,0:T(8,128)}, u32[]{:S(2)}) copy-start(f32[1,512,8]{1,2,0:T(8,128)} %param.24) | copy-start | bytes 49156
  232.9 19.2 %all-to-all-start = ((bf16[4,192,768]{2,1,0:T(8,128)(2,1)}), bf16[4,192,768]{2,1,0:T(8,128)(2,1)}, u32[]{:S(2)}, u32[]{:S(2)}) async-start(bf16[4,192,768]{2,1,0:T(8,128)(2,1)} %fusion.40), calls=%async_computation.1 | async-start | bytes 2359296 | tf_op jit(solution)/shard_map/all_to_all | solution.py:156
  380.5 1.1 copy-start.3
Sparse Core Ops, SparseCore 0:
  11.9 29.8 all-gather.11
  197.0 26.0 reduce-scatter.1
Sparse Core Ops, SparseCore 1:
  199.6 45.5 all-gather.5
  247.3 43.7 all-gather.9
  293.5 43.7 all-gather.7
where the time goes:
time: 392 us; the launch traced here: 390 us
  waiting for transfers between devices  142 us (36%)
  matrix products  93.9 us (24%)
  other arithmetic  54.2 us (14%)
  local copies, waits for them, and re-layouts  43.3 us (11%)
  blocking collectives  30.4 us (8%)
  between operations  17.8 us (5%)
  starting transfers between devices  4.8 us (1%)
    all_gather x1, waiting for transfers between devices, on_device(): lax.all_gather(expert_up, 'req', axis=1, tiled=True)  46.1 us
    dot_general x5, matrix products, visit(): jnp.einsum('kqd,kjd->kqj', query, key_block, preferred_element_type=jnp.f...  40.3 us
    reduce_sum x5, other arithmetic, visit(): total = total * correction + jnp.sum(probs, -1)  34.3 us
    all_gather x1, waiting for transfers between devices, on_device(): lax.all_gather(expert_down, 'req', axis=1, tiled=True)  32.5 us
    dot_general x5, matrix products, visit(): jnp.einsum('kqj,kjd->kqd', probs.astype(jnp.bfloat16), value_block, prefe...  29.5 us
    all_to_all x1, blocking collectives, on_device(): lax.all_to_all(contrib, 'ep', split_axis=2, concat_axis=0, tiled=True)  25.2 us
    all_gather x1, waiting for transfers between devices, on_device(): rows_whole = lax.all_gather(own_rows, 'ep', axis=1, tiled=True)  25.2 us
    reduce_scatter x1, waiting for transfers between devices, on_device(): lax.psum_scatter(partial_value.astype(jnp.bfloat16), 'ep', scatter_dimens...  22.6 us
  transfers between devices with their start and end apart: 6, of which 5 were waited for; matrix products, arithmetic and copies ran while one was open for 4% of the time, Pallas kernels for 0%

commit v1 on v0

--- a/solution.py
+++ b/solution.py
@@ -177,7 +177,10 @@
         preferred_element_type=jnp.float32,
     )
     contrib = (output * gate_own[..., None]).astype(jnp.bfloat16)
-    returned = lax.all_to_all(contrib, "ep", split_axis=2, concat_axis=0, tiled=True)
+    returned = jnp.concatenate(
+        lax.all_to_all(jnp.stack(jnp.split(contrib, lax.axis_size("ep"), axis=2)), "ep", 0, 0),
+        axis=0,
+    )
     per_expert = jnp.einsum("ect,ecd->etd", table_all, returned, preferred_element_type=jnp.float32)
     grouped = rounded(jnp.sum(per_expert.reshape(devices, per_device, new_rows, own_width), 1))
     expert_sum = jnp.sum(grouped, 0)

time: 392 us -> 375 us (0.957)
  local copies, waits for them, and re-layouts: 43.3 us -> 34.9 us
  blocking collectives: 30.4 us -> 23.3 us
    all_to_all x1, blocking collectives: 25.2 us -> 18.2 us  [on_device(): lax.all_to_all(jnp.stack(jnp.split(contrib, lax.axis_size('ep'), axis=2))...]
    all_to_all x1 -> x0, local copies, waits for them, and re-layouts: 4.89 us -> none  [on_device(): lax.all_to_all(contrib, 'ep', split_axis=2, concat_axis=0, tiled=True)]
    convert_element_type x1 -> x0, local copies, waits for them, and re-layouts: 4.83 us -> none  [on_device(): contrib = (output * gate_own[..., None]).astype(jnp.bfloat16)]
where the time goes in v1:
time: 375 us; the launch traced here: 374 us
  waiting for transfers between devices  142 us (38%)
  matrix products  92.5 us (25%)
  other arithmetic  54.3 us (14%)
  local copies, waits for them, and re-layouts  34.9 us (9%)
  blocking collectives  23.3 us (6%)
  between operations  17.8 us (5%)
  starting transfers between devices  4.8 us (1%)
    all_gather x1, waiting for transfers between devices, on_device(): lax.all_gather(expert_up, 'req', axis=1, tiled=True)  46.1 us
    dot_general x5, matrix products, visit(): jnp.einsum('kqd,kjd->kqj', query, key_block, preferred_element_type=jnp.f...  40.3 us
    reduce_sum x5, other arithmetic, visit(): total = total * correction + jnp.sum(probs, -1)  34.3 us
    all_gather x1, waiting for transfers between devices, on_device(): lax.all_gather(expert_down, 'req', axis=1, tiled=True)  32.5 us
    dot_general x5, matrix products, visit(): jnp.einsum('kqj,kjd->kqd', probs.astype(jnp.bfloat16), value_block, prefe...  29.5 us
    all_gather x1, waiting for transfers between devices, on_device(): rows_whole = lax.all_gather(own_rows, 'ep', axis=1, tiled=True)  25.2 us
    reduce_scatter x1, waiting for transfers between devices, on_device(): lax.psum_scatter(partial_value.astype(jnp.bfloat16), 'ep', scatter_dimens...  22.6 us
    all_to_all x1, blocking collectives, on_device(): lax.all_to_all(jnp.stack(jnp.split(contrib, lax.axis_size('ep'), axis=2))...  18.2 us
  transfers between devices with their start and end apart: 6, of which 5 were waited for; matrix products, arithmetic and copies ran while one was open for 4% of the time, Pallas kernels for 0%

profile of v1, /device:TPU:0, one launch (start us, length us, event | category | flops | bytes accessed | tf_op | source)
XLA Modules:
  0.0 373.6 jit_solution(6762870034929929859)
XLA Ops:
  8.1 2.6 copy.65
  16.7 25.2 %all-gather.12.cloned.1.call-done = bf16[1,512,1536]{2,1,0:T(8,128)(2,1)} async-done(((bf16[1,512,768]{2,1,0:T(8,128)(2,1)}), bf16[1,512,1536]{2,1,0:T(8,128)(2,1)}) %all-gather.12.cloned.1.call-update) | async-done | bytes 1572880 | tf_op jit(solution)/shard_map/all_gather | solution.py:108
  54.8 4.0 %dynamic_update_slice.6 = bf16[4,2560,64]{1,2,0:T(8,128)(2,1)} dynamic-update-slice(bf16[4,2560,64]{1,2,0:T(8,128)(2,1)} %bitcast.102, bf16[4,512,64]{1,2,0:T(8,128)(2,1)S(1)} %pad_maximum_fusion.2, s32[]{:T(128)} %constant.31.clone.1, s32[]{:T(128)S(6)} %select_n.46, s32[]{:T(128)} %constant.31.clone.1) | dynamic-update-slice | bytes 524292 | tf_op jit(solution)/shard_map/dynamic_update_slice | solution.py:126
  61.1 3.8 %dynamic_update_slice.7 = bf16[4,2560,64]{1,2,0:T(8,128)(2,1)} dynamic-update-slice(bf16[4,2560,64]{1,2,0:T(8,128)(2,1)} %bitcast.109, bf16[4,512,64]{1,2,0:T(8,128)(2,1)S(1)} %bitcast.113, s32[]{:T(128)} %constant.31.clone.1, s32[]{:T(128)S(6)} %select_n.46, s32[]{:T(128)} %constant.31.clone.1) | dynamic-update-slice | bytes 524292 | tf_op jit(solution)/shard_map/dynamic_update_slice | solution.py:127
  64.9 123.9 %while.15 = (s32[]{:T(128)}, f32[4,1536]{1,0:T(4,128)S(1)}, f32[4,1536]{1,0:T(4,128)S(1)}, f32[4,1536,64]{1,2,0:T(8,128)}, s32[5]{0:T(128)S(1)}, /*index=5*/bf16...) while((s32[]{:T(128)}, f32[4,1536]{1,0:T(4,128)S(1)}, ...), condition=%wide.region_6.7_spmd.clone, body=%wide.region_3.6_spmd.clone.sunk | while | flops 848208896 | bytes 96092400 | solution.py:73
  67.5 8.1 %fusion.93 = (f32[4,1536]{1,0:T(4,128)S(1)}, f32[4,512,1536]{2,1,0:T(8,128)}) fusion(pred[1536,512]{0,1:T(8,128)(4,1)S(1)} %broadcast_compare_fusion.3, bf16[4,1536,64]{1,2,0:T(8,128)(2,1)} %get-tuple-element.229, bf16[4,2560,64]{1,2,0:T(8,128)(2,1)} %get-tuple-element.228, s32[]{:T(128)S(6)} %select_n.102), kind=kOutput, calls=%fused_computation.3.clone.1 | convolution fusion | flops 412084224 | bytes 14442500 | tf_op jit(solution)/shard_map/while/body/eval_jaxpr/kqd,kjd->kqj/dot_general | solution.py:51
  75.6 6.9 %fusion.94 = f32[4,1536]{1,0:T(4,128)S(1)} fusion(f32[4,512,1536]{2,1,0:T(8,128)} %get-tuple-element.194, f32[4,1536]{1,0:T(4,128)S(1)} %select_maximum_fusion.2, pred[1536,512]{0,1:T(8,128)(4,1)S(1)} %broadcast_compare_fusion.3), kind=kLoop, calls=%fused_computation.5.clone.1 | loop fusion | flops 15722496 | bytes 13418496 | tf_op jit(solution)/shard_map/while/body/eval_jaxpr/reduce_sum | solution.py:59
  83.8 5.7 %fusion.96 = f32[4,1536,64]{1,2,0:T(8,128)} fusion(f32[4,512,1536]{2,1,0:T(8,128)S(1)} %copy-done.1, f32[4,1536]{1,0:T(4,128)S(1)} %select_maximum_fusion.2, pred[1536,512]{0,1:T(8,128)(4,1)S(1)} %broadcast_compare_fusion.3, f32[4,1536,64]{1,2,0:T(8,128)} %get-tuple-element.213, f32[4,1536]{1,0:T(4,128)S(1)} %get-tuple-element.196, pred[]{:T(512)S(6)} %compare.4, ...), kind=kOutput, calls=%fused_computation.8.clone.1 | convolution fusion | flops 419561472 | bytes 16826372 | tf_op jit(solution)/shard_map/while/body/eval_jaxpr/kqj,kjd->kqd/dot_general | solution.py:60
  92.1 8.1 %fusion.93 = (f32[4,1536]{1,0:T(4,128)S(1)}, f32[4,512,1536]{2,1,0:T(8,128)}) fusion(pred[1536,512]{0,1:T(8,128)(4,1)S(1)} %broadcast_compare_fusion.3, bf16[4,1536,64]{1,2,0:T(8,128)(2,1)} %get-tuple-element.229, bf16[4,2560,64]{1,2,0:T(8,128)(2,1)} %get-tuple-element.228, s32[]{:T(128)S(6)} %select_n.102), kind=kOutput, calls=%fused_computation.3.clone.1 | convolution fusion | flops 412084224 | bytes 14442500 | tf_op jit(solution)/shard_map/while/body/eval_jaxpr/kqd,kjd->kqj/dot_general | solution.py:51
  100.1 6.9 %fusion.94 = f32[4,1536]{1,0:T(4,128)S(1)} fusion(f32[4,512,1536]{2,1,0:T(8,128)} %get-tuple-element.194, f32[4,1536]{1,0:T(4,128)S(1)} %select_maximum_fusion.2, pred[1536,512]{0,1:T(8,128)(4,1)S(1)} %broadcast_compare_fusion.3), kind=kLoop, calls=%fused_computation.5.clone.1 | loop fusion | flops 15722496 | bytes 13418496 | tf_op jit(solution)/shard_map/while/body/eval_jaxpr/reduce_sum | solution.py:59
  108.4 6.0 %fusion.96 = f32[4,1536,64]{1,2,0:T(8,128)} fusion(f32[4,512,1536]{2,1,0:T(8,128)S(1)} %copy-done.1, f32[4,1536]{1,0:T(4,128)S(1)} %select_maximum_fusion.2, pred[1536,512]{0,1:T(8,128)(4,1)S(1)} %broadcast_compare_fusion.3, f32[4,1536,64]{1,2,0:T(8,128)} %get-tuple-element.213, f32[4,1536]{1,0:T(4,128)S(1)} %get-tuple-element.196, pred[]{:T(512)S(6)} %compare.4, ...), kind=kOutput, calls=%fused_computation.8.clone.1 | convolution fusion | flops 419561472 | bytes 16826372 | tf_op jit(solution)/shard_map/while/body/eval_jaxpr/kqj,kjd->kqd/dot_general | solution.py:60
  116.9 8.1 %fusion.93 = (f32[4,1536]{1,0:T(4,128)S(1)}, f32[4,512,1536]{2,1,0:T(8,128)}) fusion(pred[1536,512]{0,1:T(8,128)(4,1)S(1)} %broadcast_compare_fusion.3, bf16[4,1536,64]{1,2,0:T(8,128)(2,1)} %get-tuple-element.229, bf16[4,2560,64]{1,2,0:T(8,128)(2,1)} %get-tuple-element.228, s32[]{:T(128)S(6)} %select_n.102), kind=kOutput, calls=%fused_computation.3.clone.1 | convolution fusion | flops 412084224 | bytes 14442500 | tf_op jit(solution)/shard_map/while/body/eval_jaxpr/kqd,kjd->kqj/dot_general | solution.py:51
  125.0 6.9 %fusion.94 = f32[4,1536]{1,0:T(4,128)S(1)} fusion(f32[4,512,1536]{2,1,0:T(8,128)} %get-tuple-element.194, f32[4,1536]{1,0:T(4,128)S(1)} %select_maximum_fusion.2, pred[1536,512]{0,1:T(8,128)(4,1)S(1)} %broadcast_compare_fusion.3), kind=kLoop, calls=%fused_computation.5.clone.1 | loop fusion | flops 15722496 | bytes 13418496 | tf_op jit(solution)/shard_map/while/body/eval_jaxpr/reduce_sum | solution.py:59
  133.2 6.0 %fusion.96 = f32[4,1536,64]{1,2,0:T(8,128)} fusion(f32[4,512,1536]{2,1,0:T(8,128)S(1)} %copy-done.1, f32[4,1536]{1,0:T(4,128)S(1)} %select_maximum_fusion.2, pred[1536,512]{0,1:T(8,128)(4,1)S(1)} %broadcast_compare_fusion.3, f32[4,1536,64]{1,2,0:T(8,128)} %get-tuple-element.213, f32[4,1536]{1,0:T(4,128)S(1)} %get-tuple-element.196, pred[]{:T(512)S(6)} %compare.4, ...), kind=kOutput, calls=%fused_computation.8.clone.1 | convolution fusion | flops 419561472 | bytes 16826372 | tf_op jit(solution)/shard_map/while/body/eval_jaxpr/kqj,kjd->kqd/dot_general | solution.py:60
  141.7 8.1 %fusion.93 = (f32[4,1536]{1,0:T(4,128)S(1)}, f32[4,512,1536]{2,1,0:T(8,128)}) fusion(pred[1536,512]{0,1:T(8,128)(4,1)S(1)} %broadcast_compare_fusion.3, bf16[4,1536,64]{1,2,0:T(8,128)(2,1)} %get-tuple-element.229, bf16[4,2560,64]{1,2,0:T(8,128)(2,1)} %get-tuple-element.228, s32[]{:T(128)S(6)} %select_n.102), kind=kOutput, calls=%fused_computation.3.clone.1 | convolution fusion | flops 412084224 | bytes 14442500 | tf_op jit(solution)/shard_map/while/body/eval_jaxpr/kqd,kjd->kqj/dot_general | solution.py:51
  149.8 6.9 %fusion.94 = f32[4,1536]{1,0:T(4,128)S(1)} fusion(f32[4,512,1536]{2,1,0:T(8,128)} %get-tuple-element.194, f32[4,1536]{1,0:T(4,128)S(1)} %select_maximum_fusion.2, pred[1536,512]{0,1:T(8,128)(4,1)S(1)} %broadcast_compare_fusion.3), kind=kLoop, calls=%fused_computation.5.clone.1 | loop fusion | flops 15722496 | bytes 13418496 | tf_op jit(solution)/shard_map/while/body/eval_jaxpr/reduce_sum | solution.py:59
  158.1 6.0 %fusion.96 = f32[4,1536,64]{1,2,0:T(8,128)} fusion(f32[4,512,1536]{2,1,0:T(8,128)S(1)} %copy-done.1, f32[4,1536]{1,0:T(4,128)S(1)} %select_maximum_fusion.2, pred[1536,512]{0,1:T(8,128)(4,1)S(1)} %broadcast_compare_fusion.3, f32[4,1536,64]{1,2,0:T(8,128)} %get-tuple-element.213, f32[4,1536]{1,0:T(4,128)S(1)} %get-tuple-element.196, pred[]{:T(512)S(6)} %compare.4, ...), kind=kOutput, calls=%fused_computation.8.clone.1 | convolution fusion | flops 419561472 | bytes 16826372 | tf_op jit(solution)/shard_map/while/body/eval_jaxpr/kqj,kjd->kqd/dot_general | solution.py:60
  166.6 8.1 %fusion.93 = (f32[4,1536]{1,0:T(4,128)S(1)}, f32[4,512,1536]{2,1,0:T(8,128)}) fusion(pred[1536,512]{0,1:T(8,128)(4,1)S(1)} %broadcast_compare_fusion.3, bf16[4,1536,64]{1,2,0:T(8,128)(2,1)} %get-tuple-element.229, bf16[4,2560,64]{1,2,0:T(8,128)(2,1)} %get-tuple-element.228, s32[]{:T(128)S(6)} %select_n.102), kind=kOutput, calls=%fused_computation.3.clone.1 | convolution fusion | flops 412084224 | bytes 14442500 | tf_op jit(solution)/shard_map/while/body/eval_jaxpr/kqd,kjd->kqj/dot_general | solution.py:51
  174.7 6.9 %fusion.94 = f32[4,1536]{1,0:T(4,128)S(1)} fusion(f32[4,512,1536]{2,1,0:T(8,128)} %get-tuple-element.194, f32[4,1536]{1,0:T(4,128)S(1)} %select_maximum_fusion.2, pred[1536,512]{0,1:T(8,128)(4,1)S(1)} %broadcast_compare_fusion.3), kind=kLoop, calls=%fused_computation.5.clone.1 | loop fusion | flops 15722496 | bytes 13418496 | tf_op jit(solution)/shard_map/while/body/eval_jaxpr/reduce_sum | solution.py:59
  182.9 6.0 %fusion.96 = f32[4,1536,64]{1,2,0:T(8,128)} fusion(f32[4,512,1536]{2,1,0:T(8,128)S(1)} %copy-done.1, f32[4,1536]{1,0:T(4,128)S(1)} %select_maximum_fusion.2, pred[1536,512]{0,1:T(8,128)(4,1)S(1)} %broadcast_compare_fusion.3, f32[4,1536,64]{1,2,0:T(8,128)} %get-tuple-element.213, f32[4,1536]{1,0:T(4,128)S(1)} %get-tuple-element.196, pred[]{:T(512)S(6)} %compare.4, ...), kind=kOutput, calls=%fused_computation.8.clone.1 | convolution fusion | flops 419561472 | bytes 16826372 | tf_op jit(solution)/shard_map/while/body/eval_jaxpr/kqj,kjd->kqd/dot_general | solution.py:60
  194.2 2.6 convolution_convert_fusion
  200.4 22.6 %reduce-scatter.2.cloned.1.call-done = bf16[512,768]{1,0:T(8,128)(2,1)} async-done(((bf16[512,1536]{1,0:T(8,128)(2,1)}), bf16[512,768]{1,0:T(8,128)(2,1)}) %reduce-scatter.2.cloned.1.call-update) | async-done | bytes 786448 | tf_op jit(solution)/shard_map/reduce_scatter | solution.py:136
  224.5 5.2 %psum.7 = f32[512]{0:T(512)S(1)} all-reduce(f32[512]{0:T(512)S(1)} %fusion.28), channel_id=1, replica_groups=mesh['req'=16,'ep'=2] {'ep'}, use_global_device_ids=true, to_apply=%region_12.13 | all-reduce | flops 512 | bytes 4096 | tf_op jit(solution)/shard_map/psum | solution.py:145
  229.7 3.2 fusion.40
  232.9 4.6 %all-to-all-start = ((bf16[4,192,768]{2,1,0:T(8,128)(2,1)}), bf16[4,192,768]{2,1,0:T(8,128)(2,1)}, u32[]{:S(2)}, u32[]{:S(2)}) async-start(bf16[4,192,768]{2,1,0:T(8,128)(2,1)} %fusion.40), calls=%async_computation.1 | async-start | bytes 2359296 | tf_op jit(solution)/shard_map/all_to_all | solution.py:156
  238.0 14.2 %all-to-all-done = bf16[4,192,768]{2,1,0:T(8,128)(2,1)} async-done(((bf16[4,192,768]{2,1,0:T(8,128)(2,1)}), bf16[4,192,768]{2,1,0:T(8,128)(2,1)}, u32[]{:S(2)}, u32[]{:S(2)}) %all-to-all-start) | async-done | bytes 1179680 | tf_op jit(solution)/shard_map/all_to_all | solution.py:156
  252.2 2.4 copy.45
  254.6 3.9 %fusion.68 = f32[2,192,512]{2,1,0:T(8,128)} fusion(bf16[2,192,1536]{2,1,0:T(8,128)(2,1)} %bitcast.104, bf16[2,1536,512]{2,1,0:T(8,128)(2,1)} %all-gather.6.cloned.1.call-done), kind=kOutput, calls=%fused_computation.103 | convolution fusion | flops 603979776 | bytes 5111808 | tf_op jit(solution)/shard_map/ecd,edf->ecf/dot_general | solution.py:159
  258.5 32.5 %all-gather.10.cloned.1.call-done = bf16[2,512,1536]{2,1,0:T(8,128)(2,1)} async-done(((bf16[2,32,1536]{2,1,0:T(8,128)(2,1)}), bf16[2,512,1536]{2,1,0:T(8,128)(2,1)}) %all-gather.10.cloned.1.call-update) | async-done | bytes 3145744 | tf_op jit(solution)/shard_map/all_gather | solution.py:176
  291.0 46.1 %all-gather.8.cloned.1.call-done = bf16[2,1536,512]{2,1,0:T(8,128)(2,1)} async-done(((bf16[2,96,512]{2,1,0:T(8,128)(2,1)}), bf16[2,1536,512]{2,1,0:T(8,128)(2,1)}) %all-gather.8.cloned.1.call-update) | async-done | bytes 3145744 | tf_op jit(solution)/shard_map/all_gather | solution.py:168
  337.2 5.9 %fusion.27 = bf16[2,192,1536]{2,1,0:T(8,128)(2,1)} fusion(bf16[2,512,1536]{2,1,0:T(8,128)(2,1)} %all-gather.10.cloned.1.call-done, f32[2,192]{1,0:T(2,128)S(1)} %constant_dynamic-slice_fusion, bf16[2,192,1536]{2,1,0:T(8,128)(2,1)} %bitcast.105, bf16[2,1536,512]{2,1,0:T(8,128)(2,1)} %all-gather.8.cloned.1.call-done, f32[2,192,512]{2,1,0:T(8,128)} %fusion.68), kind=kOutput, calls=%fused_computation.39 | convolution fusion | flops 1210318848 | bytes 9438720 | tf_op jit(solution)/shard_map/ecf,efd->ecd/dot_general | solution.py:173
  344.5 18.2 %all_to_all.23 = bf16[2,2,192,768]{3,2,1,0:T(8,128)(2,1)S(1)} all-to-all(bf16[2,2,192,768]{3,2,1,0:T(8,128)(2,1)S(1)} %pad_maximum_fusion), channel_id=1, replica_groups=mesh['req'=16,'ep'=2] {'ep'}, dimensions={0} | all-to-all | bytes 2359296 | tf_op jit(solution)/shard_map/all_to_all | solution.py:181
  (127 shorter events, 51.0 us)
Async XLA Ops:
  8.0 186.2 %copy-start = (bf16[768,1536]{1,0:T(8,128)(2,1)S(1)}, bf16[768,1536]{1,0:T(8,128)(2,1)}, u32[]{:S(2)}) copy-start(bf16[768,1536]{1,0:T(8,128)(2,1)} %param.30) | copy-start | bytes 7077892
  8.0 33.8 %all-gather.12.cloned.1.call-start = ((), (), s32[]{:S(2)}) async-start(), calls=%async_computation.7 | async-start | bytes 2359296 | tf_op jit(solution)/shard_map/all_gather | solution.py:108
  8.1 2.6 copy-start.5
  10.7 1.2 copy-start.11
  10.7 1.8 copy-start.12
  11.8 32.0 %copy-start.10 = (f32[1536]{0:T(1024)S(1)}, f32[1536]{0:T(1024)}, u32[]{:S(2)}) copy-start(f32[1536]{0:T(1024)} %param.25) | copy-start | bytes 18436
  11.8 211.3 %reduce-scatter.2.cloned.1.call-start = ((), (), s32[]{:S(2)}) async-start(), calls=%async_computation.3 | async-start | bytes 2359296 | tf_op jit(solution)/shard_map/reduce_scatter | solution.py:136
  41.8 1.9 copy-start.4
  43.8 2.2 copy-start.9
  75.6 8.3 %copy-start.1 = (f32[4,512,1536]{2,1,0:T(8,128)S(1)}, f32[4,512,1536]{2,1,0:T(8,128)}, u32[]{:S(2)}) copy-start(f32[4,512,1536]{2,1,0:T(8,128)} %get-tuple-element.194) | copy-start | bytes 37748740 | tf_op jit(solution)/shard_map/while
  100.1 8.3 %copy-start.1 = (f32[4,512,1536]{2,1,0:T(8,128)S(1)}, f32[4,512,1536]{2,1,0:T(8,128)}, u32[]{:S(2)}) copy-start(f32[4,512,1536]{2,1,0:T(8,128)} %get-tuple-element.194) | copy-start | bytes 37748740 | tf_op jit(solution)/shard_map/while
  125.0 8.3 %copy-start.1 = (f32[4,512,1536]{2,1,0:T(8,128)S(1)}, f32[4,512,1536]{2,1,0:T(8,128)}, u32[]{:S(2)}) copy-start(f32[4,512,1536]{2,1,0:T(8,128)} %get-tuple-element.194) | copy-start | bytes 37748740 | tf_op jit(solution)/shard_map/while
  149.8 8.3 %copy-start.1 = (f32[4,512,1536]{2,1,0:T(8,128)S(1)}, f32[4,512,1536]{2,1,0:T(8,128)}, u32[]{:S(2)}) copy-start(f32[4,512,1536]{2,1,0:T(8,128)} %get-tuple-element.194) | copy-start | bytes 37748740 | tf_op jit(solution)/shard_map/while
  174.7 8.3 %copy-start.1 = (f32[4,512,1536]{2,1,0:T(8,128)S(1)}, f32[4,512,1536]{2,1,0:T(8,128)}, u32[]{:S(2)}) copy-start(f32[4,512,1536]{2,1,0:T(8,128)} %get-tuple-element.194) | copy-start | bytes 37748740 | tf_op jit(solution)/shard_map/while
  196.8 1.8 copy-start.6
  196.8 3.5 copy-start.8
  196.8 26.3 %copy-start.2 = (bf16[1,512,768]{2,1,0:T(8,128)(2,1)S(1)}, bf16[1,512,768]{2,1,0:T(8,128)(2,1)}, u32[]{:S(2)}) copy-start(bf16[1,512,768]{2,1,0:T(8,128)(2,1)} %param.18) | copy-start | bytes 2359300
  196.8 57.7 %all-gather.6.cloned.1.call-start = ((), (), s32[]{:S(2)}) async-start(), calls=%async_computation.4 | async-start | bytes 3342336 | tf_op jit(solution)/shard_map/all_gather | solution.py:162
  197.4 93.6 %all-gather.10.cloned.1.call-start = ((), (), s32[]{:S(2)}) async-start(), calls=%async_computation.6 | async-start | bytes 3342336 | tf_op jit(solution)/shard_map/all_gather | solution.py:176
  198.0 139.2 %all-gather.8.cloned.1.call-start = ((), (), s32[]{:S(2)}) async-start(), calls=%async_computation.5 | async-start | bytes 3342336 | tf_op jit(solution)/shard_map/all_gather | solution.py:168
  232.9 4.6 %copy-start.7 = (f32[1,512,8]{1,2,0:T(8,128)S(1)}, f32[1,512,8]{1,2,0:T(8,128)}, u32[]{:S(2)}) copy-start(f32[1,512,8]{1,2,0:T(8,128)} %param.24) | copy-start | bytes 49156
  232.9 19.2 %all-to-all-start = ((bf16[4,192,768]{2,1,0:T(8,128)(2,1)}), bf16[4,192,768]{2,1,0:T(8,128)(2,1)}, u32[]{:S(2)}, u32[]{:S(2)}) async-start(bf16[4,192,768]{2,1,0:T(8,128)(2,1)} %fusion.40), calls=%async_computation.1 | async-start | bytes 2359296 | tf_op jit(solution)/shard_map/all_to_all | solution.py:156
  363.7 1.1 copy-start.3
Sparse Core Ops, SparseCore 0:
  11.9 29.8 all-gather.11
  197.0 26.0 reduce-scatter.1
Sparse Core Ops, SparseCore 1:
  199.6 45.5 all-gather.5
  247.3 43.7 all-gather.9
  293.5 43.7 all-gather.7
